TPU v7x, 32 devices: a whole 2x2x4 slice. The times are simulated.
32 devices in a mesh: well: 4 (over y, x), tile: 8 (over z, core).
Axes of the slice: x: 2, y: 2, z: 4, core: 2. Of those that a mesh axis runs over, the one named last changes fastest.
Arguments:
- prior_state: float32 [3, 200, 8192], P(None, None, 'tile'), may hold values from -6 to 6
- pred_data: float32 [4096, 200], P(('well', 'tile')), may hold values from -6 to 6
- obs_pert: float32 [4096, 200], P(('well', 'tile')), may hold values from -12 to 12
- obs_std: float32 [4096], P(('well', 'tile')), may hold values from 0.5 to 2
- loc_mask: int32 [8, 32], P('tile', 'well'), may hold values from 0 to 1, as said below
- taper_level: int32 [8, 32], P('tile', 'well'), may hold values from 1 to 4
Outputs:
- analysis: float32 [3, 200, 8192], P(None, 'well', 'tile')
Inputs may be any that keep to these rules, and one draw needn't show every extreme that they name: `loc_mask`: each tile is localized to a set of data blocks whose size varies strongly from tile to tile; some tile is localized to most blocks.
All inputs are finite; a program needn't handle non-finite values.
Results may differ from a plain program's by a relative error of at most 0.0003.
Values sent between devices are 32-bit elements; how exact they have to be, the bound alone decides.
No kernel may reach another device: no remote copies, remote signals or barrier semaphores. Data moves between devices by JAX's collectives and lax.ppermute only.
A program may use at most 64 MiB of HBM per device.

v0:
```python
import jax
import jax.numpy as jnp
from jax import lax
from jax.sharding import PartitionSpec as P

BLOCK = 128


def chol_apply(system, right):
    factor = jnp.linalg.cholesky(system)
    middle = lax.linalg.triangular_solve(
        factor, right, left_side=True, lower=True, transpose_a=False
    )
    return lax.linalg.triangular_solve(factor, middle, left_side=True, lower=True, transpose_a=True)


def prepare(pred_rows, obs_rows, std_rows, norm_factor):
    data_anom = (pred_rows - jnp.mean(pred_rows, axis=1, keepdims=True)) * norm_factor
    innov = obs_rows - pred_rows
    row_weight = 1.0 / (4.0 * std_rows * std_rows)
    scaled = row_weight[:, None] * data_anom
    return (data_anom, innov, row_weight, scaled)


def shards(prior_state, pred_data, obs_pert, obs_std, loc_mask, taper_level):
    highest = lax.Precision.HIGHEST
    members = pred_data.shape[1]
    norm_factor = 1.0 / jnp.sqrt(jnp.float32(members - 1))
    data_anom, innov, row_weight, scaled = prepare(pred_data, obs_pert, obs_std, norm_factor)
    gram_matrix, cross_matrix = lax.psum(
        (
            jnp.dot(data_anom.T, scaled, precision=highest),
            jnp.dot(scaled.T, innov, precision=highest),
        ),
        ("well", "tile"),
    )
    system = jnp.eye(members, dtype=jnp.float32) + gram_matrix
    solved = chol_apply(system, cross_matrix)
    gain_rows = row_weight[:, None] * innov - jnp.dot(scaled, solved, precision=highest)
    group_anom, group_gain = (
        lax.all_gather(data_anom, "tile", axis=0, tiled=True),
        lax.all_gather(gain_rows, "tile", axis=0, tiled=True),
    )
    taper_row = loc_mask[0].astype(jnp.float32) * taper_level[0].astype(jnp.float32) / 4.0
    state_anom = (prior_state - jnp.mean(prior_state, axis=1, keepdims=True)) * norm_factor
    own_count = members // lax.axis_size("well")
    own_start = lax.axis_index("well") * own_count
    row_taper = jnp.repeat(taper_row, BLOCK)
    space = jnp.dot((group_anom * row_taper[:, None]).T, group_gain, precision=highest)
    space_mine = lax.psum_scatter(space, "well", scatter_dimension=1, tiled=True)
    increment = jnp.einsum("vnc,nm->vmc", state_anom, space_mine, precision=highest)
    prior_mine = lax.dynamic_slice_in_dim(prior_state, own_start, own_count, 1)
    return prior_mine + increment


def solution(mesh):
    return jax.shard_map(
        shards,
        mesh=mesh,
        in_specs=(
            P(None, None, "tile"),
            P(("well", "tile"), None),
            P(("well", "tile"), None),
            P(("well", "tile")),
            P("tile", "well"),
            P("tile", "well"),
        ),
        out_specs=P(None, "well", "tile"),
        check_vma=False,
    )
```

profile of v0, /device:TPU:4, one launch (start us, length us, event | category | flops | bytes accessed | tf_op | source)
XLA Modules:
  0.0 278.2 jit_solution(14750965140446197229)
XLA Ops:
  6.5 0.0 copy-start.9
  6.5 0.0 copy-start.8
  6.5 0.0 copy-start
  6.5 0.0 all-reduce.8.cloned.1.call-start
  6.5 1.1 reduce_sum.18
  7.6 1.2 broadcast_multiply_fusion.1
  8.8 0.0 copy-start.6
  8.8 2.0 fusion.22
  10.8 0.0 copy-done.6
  10.8 2.0 fusion.21
  12.8 0.0 all-reduce.8.cloned.1.call-update
  12.9 0.9 subtract_multiply_fusion.1
  13.8 16.0 %all_gather.6 = f32[1024,200]{0,1:T(8,128)S(1)} all-gather(f32[128,200]{0,1:T(8,128)S(1)} %subtract_multiply_fusion.1), channel_id=1, replica_groups=mesh['well'=4,'tile'=8] {'tile'}, dimensions={0}, use_global_device_ids=true | all-gather | bytes 921600 | tf_op jit(solution)/shard_map/all_gather | solution.py:41
  29.8 0.0 copy-done.9
  29.8 0.0 copy-done.8
  29.8 0.1 broadcast_bitcast_fusion
  29.9 0.0 copy-done
  29.9 0.8 reduce_sum.19
  30.6 110.1 %all-reduce.8.cloned.1.call-done = (f32[200,200]{1,0:T(8,128)}, f32[200,200]{0,1:T(8,128)}) async-done(((f32[200,200]{1,0:T(8,128)}, f32[200,200]{0,1:T(8,128)}), (f32[200,200]{1,0:T(8,128)}, f32[200,200]{0,1:T(8,128)})) %all-reduce.8.cloned.1.call-update) | async-done | bytes 320016 | tf_op jit(solution)/shard_map/psum | solution.py:30
  140.7 0.0 copy-start.1
  140.7 0.0 copy-start.4
  140.7 1.7 convert_add_fusion
  142.4 1.7 copy.10
  144.1 1.1 fusion.18
  145.2 0.0 copy-start.3
  145.2 0.7 copy-done.3
  145.9 0.6 cholesky.124
  146.5 13.2 %cholesky.51 = f32[128,128]{1,0:T(8,128)} custom-call(f32[128,128]{1,0:T(8,128)} %cholesky.124), custom_call_target="Cholesky" | custom-call | tf_op jit(solution)/shard_map/jit(cholesky)/cholesky | solution.py:10
  159.7 2.0 select_reduce_fusion
  161.7 1.5 cholesky.119
  163.2 11.3 %custom-call.16 = f32[1,128,128]{1,2,0:T(8,128)} custom-call(f32[1,128,128]{2,1,0:T(8,128)} %get-tuple-element.30), custom_call_target="InvertDiagBlocksLowerTriangular" | custom-call | tf_op jit(solution)/shard_map/jit(cholesky)/cholesky | solution.py:10
  174.5 1.7 constant_dynamic-update-slice_fusion.1
  176.2 1.6 convolution_subtract_fusion.3
  177.8 8.0 %cholesky.110 = f32[72,72]{1,0:T(8,128)} custom-call(f32[72,72]{1,0:T(8,128)} %convolution_subtract_fusion.3), custom_call_target="Cholesky" | custom-call | tf_op jit(solution)/shard_map/jit(cholesky)/cholesky | solution.py:10
  185.7 1.4 select_reduce_fusion.1
  187.1 0.6 compare_reduce_fusion
  187.8 1.3 compare_reduce_fusion.1
  190.3 1.0 select_select_fusion
  191.2 0.0 copy-start.2
  191.3 0.7 copy-done.2
  191.9 0.1 fusion.23
  192.0 0.7 pad_maximum_fusion
  192.7 21.1 %custom-call.17 = f32[2,128,128]{1,2,0:T(8,128)} custom-call(f32[2,128,128]{2,1,0:T(8,128)} %pad_maximum_fusion), custom_call_target="InvertDiagBlocksLowerTriangular" | custom-call | tf_op jit(solution)/shard_map/triangular_solve | solution.py:14
  213.8 1.4 fusion.19
  215.1 0.0 copy-start.5
  215.1 0.0 copy-start.7
  215.2 1.2 convolution_subtract_fusion.2
  216.4 1.0 fusion.36
  217.4 1.0 fusion.35
  218.4 1.1 convolution_subtract_fusion
  219.6 1.2 fusion.26
  220.8 0.0 copy-done.1
  220.8 0.0 copy-done.4
  220.8 1.2 convolution_subtract_fusion.1
  222.0 17.3 %all_gather.7 = f32[1024,200]{0,1:T(8,128)S(1)} all-gather(f32[128,200]{0,1:T(8,128)S(1)} %convolution_subtract_fusion.1), channel_id=1, replica_groups=mesh['well'=4,'tile'=8] {'tile'}, dimensions={0}, use_global_device_ids=true | all-gather | bytes 921600 | tf_op jit(solution)/shard_map/all_gather | solution.py:42
  239.3 0.9 fusion.12
  240.2 21.4 %fusion = f32[200,64]{0,1:T(8,128)S(1)} fusion(f32[200,200]{0,1:T(8,128)S(1)} %fusion.12), kind=kCustom, calls=%all-reduce-scatter | all-reduce-scatter fusion | flops 51201 | bytes 211712
  261.7 3.4 %collective-permute-start = (f32[200,42]{0,1:T(8,128)S(1)}, f32[200,42]{0,1:T(8,128)S(1)}, u32[]{:S(2)}, u32[]{:S(2)}) collective-permute-start(f32[200,42]{0,1:T(8,128)S(1)} %slice.74), channel_id=1, source_target_pairs={{0,8},{8,16},{16,24},{1,9},{9,17},{17,25},{2,10},{10,18},{18,26},{... | collective-permute-start | bytes 100808
  265.0 0.0 copy-done.5
  265.1 0.0 copy-done.7
  265.1 0.6 dynamic-slice.8
  266.3 2.2 collective-permute-done
  268.5 0.2 concatenate.13
  268.7 2.6 fusion.7
  (7 shorter events, 0.0 us)
Async XLA Ops:
  6.5 23.3 %copy-start.9 = (s32[1,8]{1,0:T(1,128)S(1)}, s32[1,8]{1,0:T(1,128)}, u32[]{:S(2)}) copy-start(s32[1,8]{1,0:T(1,128)} %param.10) | copy-start | bytes 100
  6.5 23.3 %copy-start.8 = (s32[1,8]{1,0:T(1,128)S(1)}, s32[1,8]{1,0:T(1,128)}, u32[]{:S(2)}) copy-start(s32[1,8]{1,0:T(1,128)} %param.11) | copy-start | bytes 100
  6.5 23.3 %copy-start = (f32[3,200,1024]{2,1,0:T(8,128)S(1)}, f32[3,200,1024]{2,1,0:T(8,128)}, u32[]{:S(2)}) copy-start(f32[3,200,1024]{2,1,0:T(8,128)} %param.6) | copy-start | bytes 7372804
  6.5 134.2 %all-reduce.8.cloned.1.call-start = ((), (), s32[]{:S(2)}) async-start(), calls=%async_computation | async-start | bytes 819200 | tf_op jit(solution)/shard_map/psum | solution.py:30
  8.8 2.0 copy-start.6
  140.7 80.0 %copy-start.1 = (f32[128,200]{0,1:T(8,128)S(1)}, f32[128,200]{0,1:T(8,128)}, u32[]{:S(2)}) copy-start(f32[128,200]{0,1:T(8,128)} %param.7) | copy-start | bytes 307204
  140.7 80.0 %copy-start.4 = (f32[128,200]{0,1:T(8,128)S(1)}, f32[128,200]{0,1:T(8,128)}, u32[]{:S(2)}) copy-start(f32[128,200]{0,1:T(8,128)} %param.8) | copy-start | bytes 307204
  145.2 0.7 copy-start.3
  191.2 0.7 copy-start.2
  215.1 49.9 %copy-start.5 = (f32[3,1024]{1,0:T(4,128)S(1)}, f32[3,1024]{1,0:T(4,128)}, u32[]{:S(2)}) copy-start(f32[3,1024]{1,0:T(4,128)} %reduce_sum.19) | copy-start | bytes 36868
  215.1 49.9 %copy-start.7 = (u32[32]{0:T(128)S(1)}, u32[32]{0:T(128)}, u32[]{:S(2)}) copy-start(u32[32]{0:T(128)} %constant.155) | copy-start | bytes 388
  261.7 6.9 %collective-permute-start = (f32[200,42]{0,1:T(8,128)S(1)}, f32[200,42]{0,1:T(8,128)S(1)}, u32[]{:S(2)}, u32[]{:S(2)}) collective-permute-start(f32[200,42]{0,1:T(8,128)S(1)} %slice.74), channel_id=1, source_target_pairs={{0,8},{8,16},{16,24},{1,9},{9,17},{17,25},{2,10},{10,18},{18,26},{... | collective-permute-start | bytes 100808
Sparse Core Ops, SparseCore 0:
  13.0 127.6 all-reduce.7
where the time goes:
time: 279 us; the launch traced here: 278 us
  waiting for transfers between devices  112 us (40%)
  other arithmetic  67.3 us (24%)
  blocking collectives  54.7 us (20%)
  matrix products  19 us (7%)
  between operations  15.4 us (6%)
  local copies, waits for them, and re-layouts  6.12 us (2%)
  starting transfers between devices  3.37 us (1%)
    psum x1, waiting for transfers between devices, shards(): lax.psum((jnp.dot(data_anom.T, scaled, precision=highest), jnp.dot(scaled...  110 us
    another operation x7, other arithmetic, chol_apply(): factor = jnp.linalg.cholesky(system)  37.8 us
    another operation x6, other arithmetic, chol_apply(): lax.linalg.triangular_solve(factor, middle, left_side=True, lower=True, t...  22.8 us
    unnamed x1, blocking collectives  21.4 us
    all_gather x1, blocking collectives, shards(): lax.all_gather(gain_rows, 'tile', axis=0, tiled=True)  17.3 us
    all_gather x1, blocking collectives, shards(): lax.all_gather(data_anom, 'tile', axis=0, tiled=True)  16 us
  transfers between devices with their start and end apart: 2, of which 2 were waited for; matrix products, arithmetic and copies ran while one was open for 1% of the time, Pallas kernels for 0%

commit v1 on v0

--- a/solution.py
+++ b/solution.py
@@ -4,6 +4,19 @@
 from jax.sharding import PartitionSpec as P
 
 BLOCK = 128
+
+
+def collect(x, axis, dim):
+    ways = lax.axis_size(axis)
+    up = [(d, (d + 1) % ways) for d in range(ways)]
+    down = [(d, (d - 1) % ways) for d in range(ways)]
+    earlier, later = ([x], [x])
+    for _ in range(ways // 2):
+        earlier.append(lax.ppermute(earlier[-1], axis, up))
+    for _ in range((ways - 1) // 2):
+        later.append(lax.ppermute(later[-1], axis, down))
+    line = jnp.concatenate([*earlier[::-1], *later[1:]], axis=dim)
+    return jnp.roll(line, (lax.axis_index(axis) - ways // 2) * x.shape[dim], axis=dim)
 
 
 def chol_apply(system, right):
@@ -38,7 +51,7 @@
     solved = chol_apply(system, cross_matrix)
     gain_rows = row_weight[:, None] * innov - jnp.dot(scaled, solved, precision=highest)
     group_anom, group_gain = (
-        lax.all_gather(data_anom, "tile", axis=0, tiled=True),
+        collect(data_anom, "tile", 0),
         lax.all_gather(gain_rows, "tile", axis=0, tiled=True),
     )
     taper_row = loc_mask[0].astype(jnp.float32) * taper_level[0].astype(jnp.float32) / 4.0

time: 279 us -> 265 us (0.950)
  waiting for transfers between devices: 112 us -> 130 us
  blocking collectives: 54.7 us -> 38.6 us
  other arithmetic: 67.3 us -> 55.6 us
  starting transfers between devices: 3.37 us -> 12.8 us
  matrix products: 19 us -> 10.5 us
  local copies, waits for them, and re-layouts: 6.12 us -> 1.16 us
    all_gather x1 -> x0, blocking collectives: 16 us -> none  [shards(): lax.all_gather(data_anom, 'tile', axis=0, tiled=True)]
    psum x1, waiting for transfers between devices: 110 us -> 120 us  [shards(): lax.psum((jnp.dot(data_anom.T, scaled, precision=highest), jnp.dot(scaled...]
    ppermute x0 -> x7, starting transfers between devices: none -> 9.46 us  [the longest x3 9.29 us: collect(): later.append(lax.ppermute(later[-1], axis, down))]
    another operation x7, other arithmetic: 37.8 us -> 29.4 us  [chol_apply(): factor = jnp.linalg.cholesky(system)]
    ppermute x0 -> x7, waiting for transfers between devices: none -> 7.41 us  [the longest x4 5.27 us: collect(): earlier.append(lax.ppermute(earlier[-1], axis, up))]
    another operation x6, other arithmetic: 22.8 us -> 19.8 us  [chol_apply(): lax.linalg.triangular_solve(factor, middle, left_side=True, lower=True, t...]
    another operation x2, matrix products: 3.27 us -> 0.42 us  [chol_apply(): factor = jnp.linalg.cholesky(system)]
  transfers between devices with their start and end apart: 2 -> 9, of which waited for: 2 -> 4; matrix products, arithmetic and copies ran while one was open for 1% -> 23% of each run, Pallas kernels for 0% -> 0%
where the time goes in v1:
time: 265 us; the launch traced here: 264 us
  waiting for transfers between devices  130 us (49%)
  other arithmetic  55.6 us (21%)
  blocking collectives  38.6 us (15%)
  between operations  15.7 us (6%)
  starting transfers between devices  12.8 us (5%)
  matrix products  10.5 us (4%)
    psum x1, waiting for transfers between devices, shards(): lax.psum((jnp.dot(data_anom.T, scaled, precision=highest), jnp.dot(scaled...  120 us
    another operation x7, other arithmetic, chol_apply(): factor = jnp.linalg.cholesky(system)  29.4 us
    unnamed x1, blocking collectives  22.3 us
    another operation x6, other arithmetic, chol_apply(): lax.linalg.triangular_solve(factor, middle, left_side=True, lower=True, t...  19.8 us
    all_gather x1, blocking collectives, shards(): lax.all_gather(gain_rows, 'tile', axis=0, tiled=True)  16.3 us
    ppermute x3, starting transfers between devices, collect(): later.append(lax.ppermute(later[-1], axis, down))  9.29 us
  transfers between devices with their start and end apart: 9, of which 4 were waited for; matrix products, arithmetic and copies ran while one was open for 23% of the time, Pallas kernels for 0%

profile of v1, /device:TPU:4, one launch (start us, length us, event | category | flops | bytes accessed | tf_op | source)
XLA Modules:
  0.0 264.3 jit_solution(15353540061912875549)
XLA Ops:
  6.5 0.0 copy-start.6
  6.5 0.0 copy-start.5
  6.5 0.0 all-reduce.8.cloned.1.call-start
  6.5 1.0 reduce_sum.18
  7.5 0.7 broadcast_multiply_fusion.1
  8.2 0.9 subtract_multiply_fusion.1
  9.1 0.1 collective-permute-start
  9.1 3.5 %collective-permute-start.4 = (f32[128,200]{0,1:T(8,128)S(1)}, f32[128,200]{0,1:T(8,128)S(1)}, u32[]{:S(2)}, u32[]{:S(2)}) collective-permute-start(f32[128,200]{0,1:T(8,128)S(1)} %subtract_multiply_fusion.1), channel_id=1, source_target_pairs={{0,7},{1,0},{2,1},{3,2},{4,3},{5,4},{6,5},{7,6},{8,15},{9,8},{10,9... | collective-permute-start | bytes 307208 | tf_op jit(solution)/shard_map/ppermute | solution.py:17
  12.7 2.0 fusion.23
  14.7 2.0 fusion.22
  16.7 0.0 all-reduce.8.cloned.1.call-update
  16.7 0.0 copy-done.6
  16.7 0.0 copy-done.5
  16.8 0.1 broadcast_bitcast_fusion
  16.8 1.9 reduce_sum.19
  18.7 0.0 collective-permute-done
  18.7 0.1 collective-permute-start.1
  18.8 0.0 collective-permute-done.4
  18.8 3.5 %collective-permute-start.5 = (f32[128,200]{0,1:T(8,128)S(1)}, f32[128,200]{0,1:T(8,128)S(1)}, u32[]{:S(2)}, u32[]{:S(2)}) collective-permute-start(f32[128,200]{0,1:T(8,128)S(1)} %collective-permute-done.4), channel_id=1, source_target_pairs={{0,7},{1,0},{2,1},{3,2},{4,3},{5,4},{6,5},{7,6},{8,15},{9,8},{10,9... | collective-permute-start | bytes 307208 | tf_op jit(solution)/shard_map/ppermute | solution.py:17
  22.3 120.2 %all-reduce.8.cloned.1.call-done = (f32[200,200]{1,0:T(8,128)}, f32[200,200]{0,1:T(8,128)}) async-done(((f32[200,200]{1,0:T(8,128)}, f32[200,200]{0,1:T(8,128)}), (f32[200,200]{1,0:T(8,128)}, f32[200,200]{0,1:T(8,128)})) %all-reduce.8.cloned.1.call-update) | async-done | bytes 320016 | tf_op jit(solution)/shard_map/psum | solution.py:43
  142.6 0.0 copy-start.3
  142.6 1.0 convert_add_fusion
  143.6 0.1 copy.10
  143.7 1.0 fusion.19
  144.7 11.7 %cholesky.51 = f32[128,128]{1,0:T(8,128)S(1)} custom-call(f32[128,128]{1,0:T(8,128)S(1)} %cholesky.124), custom_call_target="Cholesky" | custom-call | tf_op jit(solution)/shard_map/jit(cholesky)/cholesky | solution.py:23
  156.4 0.0 copy-start.2
  156.5 9.8 %custom-call.16 = f32[1,128,128]{1,2,0:T(8,128)S(1)} custom-call(f32[1,128,128]{2,1,0:T(8,128)S(1)} %get-tuple-element.30), custom_call_target="InvertDiagBlocksLowerTriangular" | custom-call | tf_op jit(solution)/shard_map/jit(cholesky)/cholesky | solution.py:23
  166.3 0.2 constant_dynamic-update-slice_fusion.16
  166.5 0.2 convolution_subtract_fusion.3
  166.7 6.6 %cholesky.110 = f32[72,72]{1,0:T(8,128)S(1)} custom-call(f32[72,72]{1,0:T(8,128)S(1)} %convolution_subtract_fusion.3), custom_call_target="Cholesky" | custom-call | tf_op jit(solution)/shard_map/jit(cholesky)/cholesky | solution.py:23
  173.3 0.6 compare_reduce_fusion
  174.0 0.6 compare_reduce_fusion.1
  175.9 0.1 fusion.24
  176.0 19.7 %custom-call.17 = f32[2,128,128]{1,2,0:T(8,128)S(1)} custom-call(f32[2,128,128]{2,1,0:T(8,128)S(1)} %pad_maximum_fusion), custom_call_target="InvertDiagBlocksLowerTriangular" | custom-call | tf_op jit(solution)/shard_map/triangular_solve | solution.py:27
  195.7 0.0 copy-done.3
  195.7 0.4 fusion.20
  196.1 0.3 convolution_subtract_fusion.2
  196.4 0.3 fusion.37
  196.7 0.2 fusion.36
  196.9 0.4 convolution_subtract_fusion
  197.3 0.3 fusion.27
  197.6 0.0 collective-permute-done.1
  197.6 0.1 collective-permute-start.2
  197.7 0.0 copy-done.1
  197.7 0.0 copy-done.2
  197.7 0.6 convolution_subtract_fusion.1
  198.3 5.3 %collective-permute-done.2 = f32[128,200]{0,1:T(8,128)S(1)} collective-permute-done((f32[128,200]{0,1:T(8,128)S(1)}, f32[128,200]{0,1:T(8,128)S(1)}, u32[]{:S(2)}, u32[]{:S(2)}) %collective-permute-start.2) | collective-permute-done | bytes 102432 | tf_op jit(solution)/shard_map/ppermute | solution.py:15
  203.6 0.0 collective-permute-start.3
  203.6 16.3 %all_gather.3 = f32[1024,200]{0,1:T(8,128)S(1)} all-gather(f32[128,200]{0,1:T(8,128)S(1)} %convolution_subtract_fusion.1), channel_id=1, replica_groups=mesh['well'=4,'tile'=8] {'tile'}, dimensions={0}, use_global_device_ids=true | all-gather | bytes 921600 | tf_op jit(solution)/shard_map/all_gather | solution.py:55
  219.9 0.0 collective-permute-done.5
  219.9 2.2 collective-permute-start.6
  222.2 0.0 collective-permute-done.3
  222.3 2.1 collective-permute-done.6
  224.5 0.0 copy-start.4
  224.5 0.0 copy-start
  224.6 0.9 fusion.12
  225.5 22.3 %fusion = f32[200,64]{0,1:T(8,128)S(1)} fusion(f32[200,200]{0,1:T(8,128)S(1)} %fusion.12), kind=kCustom, calls=%all-reduce-scatter | all-reduce-scatter fusion | flops 51201 | bytes 211712
  247.8 3.4 %collective-permute-start.7 = (f32[200,42]{0,1:T(8,128)S(1)}, f32[200,42]{0,1:T(8,128)S(1)}, u32[]{:S(2)}, u32[]{:S(2)}) collective-permute-start(f32[200,42]{0,1:T(8,128)S(1)} %slice.74), channel_id=1, source_target_pairs={{0,8},{8,16},{16,24},{1,9},{9,17},{17,25},{2,10},{10,18},{18,26},{... | collective-permute-start | bytes 100808
  251.2 0.0 copy-done.4
  251.2 0.6 dynamic-slice.8
  252.4 2.2 collective-permute-done.7
  254.6 0.2 concatenate.20
  254.8 0.0 copy-done
  254.9 2.6 %fusion.7 = f32[3,50,1024]{2,1,0:T(8,128)} fusion(f32[3,200,1024]{2,1,0:T(8,128)S(1)} %copy-done, f32[3,1024]{1,0:T(4,128)S(1)} %broadcast_multiply_fusion, s32[]{:T(128)S(6)} %select_n.20, f32[200,106]{0,1:T(8,128)S(1)} %concatenate.20, u32[]{:S(6)} %subtract.8), kind=kOutput, calls=%fused_computation.4 | convolution fusion | flops 370022400 | bytes 3833864 | tf_op jit(solution)/shard_map/vnc,nm->vmc/dot_general | solution.py:64
  (30 shorter events, 0.3 us)
Async XLA Ops:
  6.5 10.2 %copy-start.6 = (s32[1,8]{1,0:T(1,128)S(1)}, s32[1,8]{1,0:T(1,128)}, u32[]{:S(2)}) copy-start(s32[1,8]{1,0:T(1,128)} %param.10) | copy-start | bytes 100
  6.5 10.2 %copy-start.5 = (s32[1,8]{1,0:T(1,128)S(1)}, s32[1,8]{1,0:T(1,128)}, u32[]{:S(2)}) copy-start(s32[1,8]{1,0:T(1,128)} %param.11) | copy-start | bytes 100
  6.5 136.0 %all-reduce.8.cloned.1.call-start = ((), (), s32[]{:S(2)}) async-start(), calls=%async_computation | async-start | bytes 819200 | tf_op jit(solution)/shard_map/psum | solution.py:43
  9.1 9.7 %collective-permute-start = (f32[128,200]{0,1:T(8,128)S(1)}, f32[128,200]{0,1:T(8,128)S(1)}, u32[]{:S(2)}, u32[]{:S(2)}) collective-permute-start(f32[128,200]{0,1:T(8,128)S(1)} %subtract_multiply_fusion.1), channel_id=1, source_target_pairs={{0,1},{1,2},{2,3},{3,4},{4,5},{5,6},{6,7},{7,0},{8,9},{9,10},{10,1... | collective-permute-start | bytes 307208 | tf_op jit(solution)/shard_map/ppermute | solution.py:15
  9.1 9.7 %collective-permute-start.4 = (f32[128,200]{0,1:T(8,128)S(1)}, f32[128,200]{0,1:T(8,128)S(1)}, u32[]{:S(2)}, u32[]{:S(2)}) collective-permute-start(f32[128,200]{0,1:T(8,128)S(1)} %subtract_multiply_fusion.1), channel_id=1, source_target_pairs={{0,7},{1,0},{2,1},{3,2},{4,3},{5,4},{6,5},{7,6},{8,15},{9,8},{10,9... | collective-permute-start | bytes 307208 | tf_op jit(solution)/shard_map/ppermute | solution.py:17
  18.7 178.9 %collective-permute-start.1 = (f32[128,200]{0,1:T(8,128)S(1)}, f32[128,200]{0,1:T(8,128)S(1)}, u32[]{:S(2)}, u32[]{:S(2)}) collective-permute-start(f32[128,200]{0,1:T(8,128)S(1)} %collective-permute-done), channel_id=1, source_target_pairs={{0,1},{1,2},{2,3},{3,4},{4,5},{5,6},{6,7},{7,0},{8,9},{9,10},{10,1... | collective-permute-start | bytes 307208 | tf_op jit(solution)/shard_map/ppermute | solution.py:15
  18.8 201.1 %collective-permute-start.5 = (f32[128,200]{0,1:T(8,128)S(1)}, f32[128,200]{0,1:T(8,128)S(1)}, u32[]{:S(2)}, u32[]{:S(2)}) collective-permute-start(f32[128,200]{0,1:T(8,128)S(1)} %collective-permute-done.4), channel_id=1, source_target_pairs={{0,7},{1,0},{2,1},{3,2},{4,3},{5,4},{6,5},{7,6},{8,15},{9,8},{10,9... | collective-permute-start | bytes 307208 | tf_op jit(solution)/shard_map/ppermute | solution.py:17
  142.6 53.1 %copy-start.3 = (f32[200,200]{1,0:T(8,128)S(1)}, f32[200,200]{1,0:T(8,128)}, u32[]{:S(2)}) copy-start(f32[200,200]{1,0:T(8,128)} %get-tuple-element.25) | copy-start | bytes 480004
  156.4 41.3 %copy-start.1 = (f32[128,200]{0,1:T(8,128)S(1)}, f32[128,200]{0,1:T(8,128)}, u32[]{:S(2)}) copy-start(f32[128,200]{0,1:T(8,128)} %param.7) | copy-start | bytes 307204
  156.4 41.3 %copy-start.2 = (f32[128,200]{0,1:T(8,128)S(1)}, f32[128,200]{0,1:T(8,128)}, u32[]{:S(2)}) copy-start(f32[128,200]{0,1:T(8,128)} %param.8) | copy-start | bytes 307204
  197.6 5.9 %collective-permute-start.2 = (f32[128,200]{0,1:T(8,128)S(1)}, f32[128,200]{0,1:T(8,128)S(1)}, u32[]{:S(2)}, u32[]{:S(2)}) collective-permute-start(f32[128,200]{0,1:T(8,128)S(1)} %collective-permute-done.1), channel_id=1, source_target_pairs={{0,1},{1,2},{2,3},{3,4},{4,5},{5,6},{6,7},{7,0},{8,9},{9,10},{10,1... | collective-permute-start | bytes 307208 | tf_op jit(solution)/shard_map/ppermute | solution.py:15
  203.6 18.6 %collective-permute-start.3 = (f32[128,200]{0,1:T(8,128)S(1)}, f32[128,200]{0,1:T(8,128)S(1)}, u32[]{:S(2)}, u32[]{:S(2)}) collective-permute-start(f32[128,200]{0,1:T(8,128)S(1)} %collective-permute-done.2), channel_id=1, source_target_pairs={{0,1},{1,2},{2,3},{3,4},{4,5},{5,6},{6,7},{7,0},{8,9},{9,10},{10,1... | collective-permute-start | bytes 307208 | tf_op jit(solution)/shard_map/ppermute | solution.py:15
  219.9 4.5 %collective-permute-start.6 = (f32[128,200]{0,1:T(8,128)S(1)}, f32[128,200]{0,1:T(8,128)S(1)}, u32[]{:S(2)}, u32[]{:S(2)}) collective-permute-start(f32[128,200]{0,1:T(8,128)S(1)} %collective-permute-done.5), channel_id=1, source_target_pairs={{0,7},{1,0},{2,1},{3,2},{4,3},{5,4},{6,5},{7,6},{8,15},{9,8},{10,9... | collective-permute-start | bytes 307208 | tf_op jit(solution)/shard_map/ppermute | solution.py:17
  224.5 26.7 %copy-start.4 = (u32[32]{0:T(128)S(1)}, u32[32]{0:T(128)}, u32[]{:S(2)}) copy-start(u32[32]{0:T(128)} %constant.183) | copy-start | bytes 388
  224.5 30.3 %copy-start = (f32[3,200,1024]{2,1,0:T(8,128)S(1)}, f32[3,200,1024]{2,1,0:T(8,128)}, u32[]{:S(2)}) copy-start(f32[3,200,1024]{2,1,0:T(8,128)} %param.6) | copy-start | bytes 7372804
  247.8 6.9 %collective-permute-start.7 = (f32[200,42]{0,1:T(8,128)S(1)}, f32[200,42]{0,1:T(8,128)S(1)}, u32[]{:S(2)}, u32[]{:S(2)}) collective-permute-start(f32[200,42]{0,1:T(8,128)S(1)} %slice.74), channel_id=1, source_target_pairs={{0,8},{8,16},{16,24},{1,9},{9,17},{17,25},{2,10},{10,18},{18,26},{... | collective-permute-start | bytes 100808
Sparse Core Ops, SparseCore 0:
  16.8 125.6 all-reduce.7
